TPU v7x, 32 devices: a whole 2x2x4 slice. The times are simulated.
32 devices in a mesh: ctx: 4 (over y, x), tp: 8 (over z, core).
Axes of the slice: x: 2, y: 2, z: 4, core: 2. Of those that a mesh axis runs over, the one named last changes fastest.
Arguments:
- resid: bfloat16 [1024, 4096], P('ctx', 'tp'), may hold values from -6 to 6
- attn_gain: bfloat16 [4096], replicated, may hold values from 0.5 to 1.5
- mlp_gain: bfloat16 [4096], replicated, may hold values from 0.5 to 1.5
- w_query: bfloat16 [4096, 4096], P(None, 'tp'), may hold values from -0.09375 to 0.09375
- w_kv: bfloat16 [4096, 1024], P(None, 'tp'), may hold values from -0.09375 to 0.09375
- w_out: bfloat16 [4096, 4096], P('tp'), may hold values from -0.09375 to 0.09375
- w_gate: bfloat16 [4096, 11008], P(None, 'tp'), may hold values from -0.09375 to 0.09375
- w_up: bfloat16 [4096, 11008], P(None, 'tp'), may hold values from -0.09375 to 0.09375
- w_down: bfloat16 [11008, 4096], P('tp'), may hold values from -0.0546875 to 0.0546875
- kv_cache: bfloat16 [32, 128, 1024], P('ctx'), may hold values from -70 to 70
- cache_len: int32 [4], replicated, may hold values from 1 to 2048
- span_len: int32 [4], replicated, may hold values from 1 to 256
- slot_req: int32 [32], P('ctx'), may hold values from 0 to 4, as said below
- slot_blk: int32 [32], P('ctx'), may hold values from 0 to 15, as said below
Outputs:
- layer_out: bfloat16 [1024, 4096], P('ctx', 'tp')
- new_kv: bfloat16 [1024, 1024], P('ctx', 'tp')
Inputs may be any that keep to these rules, and one draw needn't show every extreme that they name: `slot_req`: each request r holds ceil(cache_len[r] / 128) blocks, and each of its blocks stands in exactly one slot; every other slot is empty. `slot_blk`: block numbers of live slots are below their request's block count; empty slots carry 0.
All inputs are finite; a program needn't handle non-finite values.
Results may differ from a plain program's by a relative error of at most 0.035.
Values may be sent and summed in bfloat16 or wider, within the bound.
No kernel may reach another device: no remote copies, remote signals or barrier semaphores. Data moves between devices by JAX's collectives and lax.ppermute only.
A program may use at most 128 MiB of HBM per device.

v0:
```python
import jax
import jax.numpy as jnp
from jax import lax
from jax.sharding import PartitionSpec as P

HQ = 32
KVH = 4
HD = 128
BLK = 128
THETA = 5000000.0
EPS = 1e-05
NEG = -1e30


def rms_norm(values, gain):
    wide = values.astype(jnp.float32)
    factor = lax.rsqrt(jnp.mean(wide * wide, axis=-1, keepdims=True) + EPS)
    return (wide * factor * gain.astype(jnp.float32)).astype(jnp.bfloat16)


def rotate(vectors, positions):
    width = vectors.shape[-1]
    half = width // 2
    freqs = THETA ** (-(jnp.arange(half, dtype=jnp.float32) * 2.0 / width))
    angles = positions.astype(jnp.float32)[:, None] * freqs[None, :]
    cosine = jnp.cos(angles)[:, None, :]
    sine = jnp.sin(angles)[:, None, :]
    first = vectors[..., :half]
    second = vectors[..., half:]
    return jnp.concatenate(
        [first * cosine - second * sine, second * cosine + first * sine], axis=-1
    )


def column_term(rows, weight):
    return lax.dot_general(
        weight, rows, (((0,), (1,)), ((), ())), preferred_element_type=jnp.float32
    )


def gather_ctx(value, count):
    parts = [value]
    for shift in range(1, count):
        pairs = [(i, (i + shift) % count) for i in range(count)]
        parts.append(lax.ppermute(value, "ctx", pairs))
    return parts


def per_device(
    resid,
    attn_gain,
    mlp_gain,
    w_query,
    w_kv,
    w_out,
    w_gate,
    w_up,
    w_down,
    kv_cache,
    cache_len,
    span_len,
    slot_req,
    slot_blk,
):
    span_size = resid.shape[0]
    ctx_count = lax.axis_size("ctx")
    q_cols = w_query.shape[1]
    heads_dev = q_cols // HD
    ctx_rank = lax.axis_index("ctx")
    tp_rank = lax.axis_index("tp")
    group = tp_rank * heads_dev // (HQ // KVH)
    my_len = cache_len[ctx_rank]
    my_span = span_len[ctx_rank]
    offsets = jnp.arange(span_size, dtype=jnp.int32)
    positions = my_len + offsets
    live_rows = offsets < my_span
    own_cache = jnp.concatenate(
        [
            lax.dynamic_slice_in_dim(kv_cache, group * HD, HD, 2),
            lax.dynamic_slice_in_dim(kv_cache, KVH * HD + group * HD, HD, 2),
        ],
        axis=2,
    )
    own_meta = jnp.stack([slot_req, slot_blk])
    cache_all = jnp.concatenate(gather_ctx(own_cache, ctx_count), axis=0)
    meta_all = jnp.concatenate(gather_ctx(own_meta, ctx_count), axis=1)
    full_resid = lax.all_gather(resid, "tp", axis=1, tiled=True)
    x_norm = rms_norm(full_resid, attn_gain)
    query = rotate(
        jnp.dot(x_norm, w_query, preferred_element_type=jnp.float32).reshape(
            span_size, heads_dev, HD
        ),
        positions,
    ).astype(jnp.bfloat16)
    kv_piece = jnp.dot(x_norm, w_kv, preferred_element_type=jnp.float32).astype(jnp.bfloat16)
    kv_width = kv_piece.shape[1]
    kv_all = lax.all_gather(kv_piece, "tp", axis=1, tiled=True)
    all_keys = rotate(
        kv_all[:, : KVH * HD].astype(jnp.float32).reshape(span_size, KVH, HD), positions
    ).astype(jnp.bfloat16)
    joined = jnp.concatenate([all_keys.reshape(span_size, KVH * HD), kv_all[:, KVH * HD :]], axis=1)
    mine = lax.dynamic_slice_in_dim(joined, tp_rank * kv_width, kv_width, 1)
    new_kv = jnp.where(live_rows[:, None], mine, jnp.zeros_like(mine))
    new_keys = lax.dynamic_index_in_dim(all_keys, group, 1, keepdims=False)
    new_vals = lax.dynamic_slice_in_dim(kv_all, KVH * HD + group * HD, HD, 1)
    cache_rows = cache_all.shape[0] * BLK
    keys = jnp.concatenate([cache_all[..., :HD].reshape(cache_rows, HD), new_keys], axis=0)
    vals = jnp.concatenate([cache_all[..., HD:].reshape(cache_rows, HD), new_vals], axis=0)
    key_pos = meta_all[1][:, None] * BLK + jnp.arange(BLK, dtype=jnp.int32)[None, :]
    cache_ok = ((meta_all[0][:, None] == ctx_rank) & (key_pos < my_len)).reshape(cache_rows)
    new_ok = (offsets[None, :] <= offsets[:, None]) & (offsets[None, :] < my_span)
    valid = jnp.concatenate(
        [jnp.broadcast_to(cache_ok[None, :], (span_size, cache_rows)), new_ok], axis=1
    )
    scores = jnp.einsum("chd,kd->hck", query, keys, preferred_element_type=jnp.float32) * HD ** (
        -0.5
    )
    peak = jnp.max(jnp.where(valid[None], scores, NEG), axis=2)
    weights = jnp.where(valid[None], jnp.exp(scores - peak[..., None]), 0.0)
    total = jnp.sum(weights, axis=2)
    summed = jnp.einsum(
        "hck,kd->hcd", weights.astype(jnp.bfloat16), vals, preferred_element_type=jnp.float32
    )
    attn_rows = (
        (summed / total[..., None])
        .transpose(1, 0, 2)
        .reshape(span_size, q_cols)
        .astype(jnp.bfloat16)
    )
    head_sum = lax.psum(
        jnp.dot(attn_rows, w_out, preferred_element_type=jnp.float32).astype(jnp.bfloat16), "tp"
    )
    full_mid = (full_resid.astype(jnp.float32) + head_sum.astype(jnp.float32)).astype(jnp.bfloat16)
    mid = lax.dynamic_slice_in_dim(full_mid, tp_rank * resid.shape[1], resid.shape[1], 1)
    x_two = rms_norm(full_mid, mlp_gain)
    gate = jnp.dot(x_two, w_gate, preferred_element_type=jnp.float32)
    up_part = jnp.dot(x_two, w_up, preferred_element_type=jnp.float32)
    hidden = (jax.nn.silu(gate) * up_part).astype(jnp.bfloat16)
    down_sum = lax.psum_scatter(
        column_term(hidden, w_down).astype(jnp.bfloat16), "tp", scatter_dimension=0, tiled=True
    ).astype(jnp.float32)
    layer_out = (mid.astype(jnp.float32) + down_sum.T).astype(jnp.bfloat16)
    layer_out = jnp.where(live_rows[:, None], layer_out, jnp.zeros_like(layer_out))
    return (layer_out, new_kv)


def solution(mesh):
    return jax.shard_map(
        per_device,
        mesh=mesh,
        in_specs=(
            P("ctx", "tp"),
            P(),
            P(),
            P(None, "tp"),
            P(None, "tp"),
            P("tp", None),
            P(None, "tp"),
            P(None, "tp"),
            P("tp", None),
            P("ctx", None, None),
            P(),
            P(),
            P("ctx"),
            P("ctx"),
        ),
        out_specs=(P("ctx", "tp"), P("ctx", "tp")),
        check_vma=False,
    )
```

profile of v0, /device:TPU:0, one launch (start us, length us, event | category | flops | bytes accessed | tf_op | source)
XLA Modules:
  0.0 248.4 jit_solution(2127436485068741131)
XLA Ops:
  8.6 3.9 %collective-permute-start.2 = (s32[2,8]{1,0:T(2,128)S(1)}, s32[2,8]{1,0:T(2,128)S(1)}, u32[]{:S(2)}, u32[]{:S(2)}) collective-permute-start(s32[2,8]{1,0:T(2,128)S(1)} %pad_add_fusion.1), channel_id=1, source_target_pairs={{0,24},{8,0},{16,8},{24,16},{1,25},{9,1},{17,9},{25,17},{2,26},{10... | collective-permute-start | bytes 200 | tf_op jit(solution)/shard_map/ppermute | solution.py:45
  14.8 2.4 collective-permute-start.5
  17.2 1.5 collective-permute-start.4
  18.7 1.2 dynamic_slice.25
  19.9 1.3 dynamic_slice.26
  26.0 5.1 %pad_add_fusion = pred[256,4352]{0,1:T(8,128)(4,1)} fusion(pred[256,256]{0,1:T(8,128)(4,1)S(1)} %fusion.45, pred[4352]{0:T(1024)(128)(4,1)S(1)} %pad.8.clone), kind=kLoop, calls=%fused_computation.20 | loop fusion | flops 1114112 | bytes 1184000 | tf_op jit(solution)/shard_map/concatenate | solution.py:112
  31.1 9.8 %collective-permute-done.4 = bf16[8,128,256]{2,1,0:T(8,128)(2,1)S(1)} collective-permute-done((bf16[8,128,256]{2,1,0:T(8,128)(2,1)S(1)}, bf16[8,128,256]{2,1,0:T(8,128)(2,1)S(1)}, u32[]{:S(2)}, u32[]{:S(2)}) %collective-permute-start.4) | collective-permute-done | bytes 524320 | tf_op jit(solution)/shard_map/ppermute | solution.py:45
  41.2 1.6 fusion.56
  42.8 1.3 copy.25
  44.1 2.2 fusion.14
  46.3 2.4 convolution_convert_fusion.2
  48.7 14.3 %all_gather.7 = bf16[256,1024]{1,0:T(8,128)(2,1)S(1)} all-gather(bf16[256,128]{1,0:T(8,128)(2,1)S(1)} %convolution_convert_fusion.2), channel_id=1, replica_groups=mesh['ctx'=4,'tp'=8] {'tp'}, dimensions={1}, use_global_device_ids=true | all-gather | bytes 589824 | tf_op jit(solution)/shard_map/all_gather | solution.py:97
  64.7 3.5 %fusion.37 = f32[256,512]{1,0:T(8,128)S(1)} fusion(bf16[4096,512]{1,0:T(8,128)(2,1)} %param.17, bf16[256,4096]{1,0:T(8,128)(2,1)S(1)} %copy-done.2, f32[4096]{0:T(1024)S(1)} %convert_element_type.74, f32[256]{0:T(256)S(1)} %add_rsqrt_fusion.1), kind=kOutput, calls=%fused_computation.43 | convolution fusion | flops 1077936128 | bytes 6833152 | tf_op jit(solution)/shard_map/dot_general | solution.py:90
  68.4 1.2 reshape.161
  72.6 8.7 %fusion.30 = f32[4352,256,4]{1,0,2:T(8,128)} fusion(bf16[256,128]{1,0:T(8,128)(2,1)S(1)} %dynamic-slice_bitcast_fusion, bf16[4096,128]{1,0:T(8,128)(2,1)S(1)} %bitcast.63, bf16[256,4,64]{2,0,1:T(8,128)(2,1)S(1)} %get-tuple-element.9, bf16[256,4,64]{2,0,1:T(8,128)(2,1)S(1)} %get-tuple-element.8), kind=kOutput, calls=%fused_computation.39 | convolution fusion | flops 1143603200 | bytes 19202048 | tf_op jit(solution)/shard_map/chd,kd->hck/dot_general | solution.py:115
  81.2 18.7 %fusion.60 = (f32[4,256]{1,0:T(4,128)S(1)}, bf16[4,256,4352]{1,2,0:T(8,128)(2,1)}) fusion(f32[4352,256,4]{1,0,2:T(8,128)} %fusion.30, pred[256,4352]{0,1:T(8,128)(4,1)} %pad_add_fusion), kind=kOutput, calls=%fused_computation.91 | output fusion | flops 31199488 | bytes 27856896 | tf_op jit(solution)/shard_map/sub | solution.py:119
  100.0 5.3 %fusion.25 = bf16[256,4,128]{0,2,1:T(8,128)(2,1)S(1)} fusion(bf16[4,256,4352]{1,2,0:T(8,128)(2,1)} %get-tuple-element.21, bf16[256,128]{0,1:T(8,128)(2,1)S(1)} %copy-done.8, bf16[4096,128]{0,1:T(8,128)(2,1)} %copy.25, f32[256,4]{0,1:T(4,128)S(1)} %bitcast.70), kind=kOutput, calls=%fused_computation.33 | convolution fusion | flops 1143341056 | bytes 10293248 | tf_op jit(solution)/shard_map/hck,kd->hcd/dot_general | solution.py:121
  105.3 2.7 %convolution_convert_fusion = bf16[256,4096]{1,0:T(8,128)(2,1)} fusion(bf16[256,512]{0,1:T(8,128)(2,1)S(1)} %bitcast.65, bf16[512,4096]{1,0:T(8,128)(2,1)S(1)} %copy-done.3), kind=kOutput, calls=%fused_computation.17 | convolution fusion | flops 1074790400 | bytes 6553600 | tf_op jit(solution)/shard_map/dot_general | solution.py:131
  108.1 63.7 %all-reduce.2.cloned.1.call-done = bf16[256,4096]{1,0:T(8,128)(2,1)} async-done(((bf16[256,4096]{1,0:T(8,128)(2,1)}), bf16[256,4096]{1,0:T(8,128)(2,1)}) %all-reduce.2.cloned.1.call-update) | async-done | bytes 2097168 | tf_op jit(solution)/shard_map/psum | solution.py:130
  171.8 3.9 %fusion.11 = (f32[256]{0:T(256)S(1)}, bf16[256,4096]{1,0:T(8,128)(2,1)}) fusion(bf16[256,4096]{1,0:T(8,128)(2,1)} %all-reduce.2.cloned.1.call-done, bf16[256,4096]{1,0:T(8,128)(2,1)S(1)} %copy-done.2), kind=kLoop, calls=%fused_computation.21 | loop fusion | flops 7339776 | bytes 6292480 | tf_op jit(solution)/shard_map/reduce_sum | solution.py:17
  175.7 7.0 %fusion.35 = f32[256,1376]{0,1:T(8,128)S(1)} fusion(bf16[4096,1376]{0,1:T(8,128)(2,1)} %param.20, bf16[256,4096]{1,0:T(8,128)(2,1)} %get-tuple-element.3, f32[4096]{0:T(1024)S(1)} %convert_element_type.87, f32[256]{0:T(256)S(1)} %add_rsqrt_fusion), kind=kOutput, calls=%fused_computation.42 | convolution fusion | flops 2889875456 | bytes 14795776 | tf_op jit(solution)/shard_map/dot_general | solution.py:136
  182.7 21.7 %fusion.10 = bf16[4096,256]{0,1:T(8,128)(2,1)} fusion(bf16[1376,4096]{1,0:T(8,128)(2,1)} %param.22, bf16[4096,1376]{0,1:T(8,128)(2,1)} %param.21, f32[256,1376]{0,1:T(8,128)S(1)} %fusion.35, bf16[256,4096]{1,0:T(8,128)(2,1)} %get-tuple-element.3, f32[4096]{0:T(1024)S(1)} %convert_element_type.87, f32[256]{0:T(256)S(1)} %add_rsqrt_fusion), kind=kOutput, calls=%fused_computation.19 | convolution fusion | flops 5778718720 | bytes 28165120 | tf_op jit(solution)/shard_map/dot_general | solution.py:36
  205.4 34.7 %reduce-scatter.2.cloned.1.call-done = bf16[512,256]{0,1:T(8,128)(2,1)} async-done(((bf16[4096,256]{0,1:T(8,128)(2,1)}), bf16[512,256]{0,1:T(8,128)(2,1)}) %reduce-scatter.2.cloned.1.call-update) | async-done | bytes 262160 | tf_op jit(solution)/shard_map/reduce_scatter | solution.py:139
  240.1 1.8 fusion.41
  (65 shorter events, 14.6 us)
Async XLA Ops:
  7.2 39.1 %copy-start = (bf16[4096,128]{1,0:T(8,128)(2,1)S(1)}, bf16[4096,128]{1,0:T(8,128)(2,1)}, u32[]{:S(2)}) copy-start(bf16[4096,128]{1,0:T(8,128)(2,1)} %param.18) | copy-start | bytes 3145732
  7.2 36.9 %all-gather.2.cloned.1.call-start = ((), (), s32[]{:S(2)}) async-start(), calls=%async_computation.1 | async-start | bytes 2359296 | tf_op jit(solution)/shard_map/all_gather | solution.py:87
  7.9 163.9 %all-reduce.2.cloned.1.call-start = ((), (), s32[]{:S(2)}) async-start(), calls=%async_computation.2 | async-start | bytes 4194304 | tf_op jit(solution)/shard_map/psum | solution.py:130
  8.6 15.9 %collective-permute-start.2 = (s32[2,8]{1,0:T(2,128)S(1)}, s32[2,8]{1,0:T(2,128)S(1)}, u32[]{:S(2)}, u32[]{:S(2)}) collective-permute-start(s32[2,8]{1,0:T(2,128)S(1)} %pad_add_fusion.1), channel_id=1, source_target_pairs={{0,24},{8,0},{16,8},{24,16},{1,25},{9,1},{17,9},{25,17},{2,26},{10... | collective-permute-start | bytes 200 | tf_op jit(solution)/shard_map/ppermute | solution.py:45
  12.5 12.0 %collective-permute-start.1 = (s32[2,8]{1,0:T(2,128)S(1)}, s32[2,8]{1,0:T(2,128)S(1)}, u32[]{:S(2)}, u32[]{:S(2)}) collective-permute-start(s32[2,8]{1,0:T(2,128)S(1)} %pad_add_fusion.1), channel_id=1, source_target_pairs={{0,16},{8,24},{16,0},{24,8},{1,17},{9,25},{17,1},{25,9},{2,18},{10... | collective-permute-start | bytes 200 | tf_op jit(solution)/shard_map/ppermute | solution.py:45
  13.0 11.5 %collective-permute-start = (s32[2,8]{1,0:T(2,128)S(1)}, s32[2,8]{1,0:T(2,128)S(1)}, u32[]{:S(2)}, u32[]{:S(2)}) collective-permute-start(s32[2,8]{1,0:T(2,128)S(1)} %pad_add_fusion.1), channel_id=1, source_target_pairs={{0,8},{8,16},{16,24},{24,0},{1,9},{9,17},{17,25},{25,1},{2,10},{10... | collective-permute-start | bytes 200 | tf_op jit(solution)/shard_map/ppermute | solution.py:45
  14.8 16.4 %collective-permute-start.5 = (bf16[8,128,256]{2,1,0:T(8,128)(2,1)S(1)}, bf16[8,128,256]{2,1,0:T(8,128)(2,1)S(1)}, u32[]{:S(2)}, u32[]{:S(2)}) collective-permute-start(bf16[8,128,256]{2,1,0:T(8,128)(2,1)S(1)} %pad_maximum_fusion.1), channel_id=1, source_target_pairs={{0,24},{8,0},{16,8},{24,16},{1,25},{9,1},{17,9},{25,17},{2,26},{10... | collective-permute-start | bytes 1572872 | tf_op jit(solution)/shard_map/ppermute | solution.py:45
  17.2 23.8 %collective-permute-start.4 = (bf16[8,128,256]{2,1,0:T(8,128)(2,1)S(1)}, bf16[8,128,256]{2,1,0:T(8,128)(2,1)S(1)}, u32[]{:S(2)}, u32[]{:S(2)}) collective-permute-start(bf16[8,128,256]{2,1,0:T(8,128)(2,1)S(1)} %pad_maximum_fusion.1), channel_id=1, source_target_pairs={{0,16},{8,24},{16,0},{24,8},{1,17},{9,25},{17,1},{25,9},{2,18},{10... | collective-permute-start | bytes 1572872 | tf_op jit(solution)/shard_map/ppermute | solution.py:45
  24.5 16.4 %collective-permute-start.3 = (bf16[8,128,256]{2,1,0:T(8,128)(2,1)S(1)}, bf16[8,128,256]{2,1,0:T(8,128)(2,1)S(1)}, u32[]{:S(2)}, u32[]{:S(2)}) collective-permute-start(bf16[8,128,256]{2,1,0:T(8,128)(2,1)S(1)} %pad_maximum_fusion.1), channel_id=1, source_target_pairs={{0,8},{8,16},{16,24},{24,0},{1,9},{9,17},{17,25},{25,1},{2,10},{10... | collective-permute-start | bytes 1572872 | tf_op jit(solution)/shard_map/ppermute | solution.py:45
  44.1 20.6 %copy-start.2 = (bf16[256,4096]{1,0:T(8,128)(2,1)S(1)}, bf16[256,4096]{1,0:T(8,128)(2,1)}, u32[]{:S(2)}) copy-start(bf16[256,4096]{1,0:T(8,128)(2,1)} %all-gather.2.cloned.1.call-done) | copy-start | bytes 6291460
  69.6 3.0 %copy-start.4 = (bf16[32,128,128]{2,1,0:T(8,128)(2,1)S(1)}, bf16[32,128,128]{2,1,0:T(8,128)(2,1)}, u32[]{:S(2)}) copy-start(bf16[32,128,128]{2,1,0:T(8,128)(2,1)} %get-tuple-element.5) | copy-start | bytes 3145732
  71.3 9.9 %copy-start.5 = (bf16[256,4,64]{2,0,1:T(8,128)(2,1)}, bf16[256,4,64]{2,0,1:T(8,128)(2,1)S(1)}, u32[]{:S(2)}) copy-start(bf16[256,4,64]{2,0,1:T(8,128)(2,1)S(1)} %get-tuple-element.11) | copy-start | bytes 393220
  81.2 18.7 %copy-start.8 = (bf16[256,128]{0,1:T(8,128)(2,1)S(1)}, bf16[256,128]{0,1:T(8,128)(2,1)}, u32[]{:S(2)}) copy-start(bf16[256,128]{0,1:T(8,128)(2,1)} %copy.21) | copy-start | bytes 196612
  100.0 5.3 %copy-start.3 = (bf16[512,4096]{1,0:T(8,128)(2,1)S(1)}, bf16[512,4096]{1,0:T(8,128)(2,1)}, u32[]{:S(2)}) copy-start(bf16[512,4096]{1,0:T(8,128)(2,1)} %param.19) | copy-start | bytes 12582916
  105.3 2.7 %copy-start.9 = (bf16[4096]{0:T(1024)(128)(2,1)S(1)}, bf16[4096]{0:T(1024)(128)(2,1)}, u32[]{:S(2)}) copy-start(bf16[4096]{0:T(1024)(128)(2,1)} %param.16) | copy-start | bytes 24580
  108.0 132.1 %reduce-scatter.2.cloned.1.call-start = ((), (), s32[]{:S(2)}) async-start(), calls=%async_computation.3 | async-start | bytes 2359296 | tf_op jit(solution)/shard_map/reduce_scatter | solution.py:139
  182.7 21.8 %copy-start.6 = (bf16[256,4,64]{2,0,1:T(8,128)(2,1)S(1)}, bf16[256,4,64]{2,0,1:T(8,128)(2,1)}, u32[]{:S(2)}) copy-start(bf16[256,4,64]{2,0,1:T(8,128)(2,1)} %copy-done.5) | copy-start | bytes 393220
  182.7 21.9 %copy-start.7 = (bf16[256,512]{1,0:T(8,128)(2,1)S(1)}, bf16[256,512]{1,0:T(8,128)(2,1)}, u32[]{:S(2)}) copy-start(bf16[256,512]{1,0:T(8,128)(2,1)} %get-tuple-element.12) | copy-start | bytes 786436
  182.7 59.2 %copy-start.1 = (bf16[4096,128]{1,0:T(8,128)(2,1)S(1)}, bf16[4096,128]{1,0:T(8,128)(2,1)}, u32[]{:S(2)}) copy-start(bf16[4096,128]{1,0:T(8,128)(2,1)} %param.18) | copy-start | bytes 3145732
Sparse Core Ops, SparseCore 0:
  9.6 31.7 all-gather.1
  108.1 63.6 all-reduce.1
  204.6 35.4 reduce-scatter.1
where the time goes:
time: 249 us; the launch traced here: 248 us
  waiting for transfers between devices  109 us (44%)
  matrix products  51.2 us (21%)
  other arithmetic  41.7 us (17%)
  blocking collectives  14.3 us (6%)
  between operations  14 us (6%)
  local copies, waits for them, and re-layouts  9.32 us (4%)
  starting transfers between devices  9.02 us (4%)
    psum x1, waiting for transfers between devices, per_device(): lax.psum(jnp.dot(attn_rows, w_out, preferred_element_type=jnp.float32).as...  63.7 us
    reduce_scatter x1, waiting for transfers between devices, per_device(): lax.psum_scatter(column_term(hidden, w_down).astype(jnp.bfloat16), 'tp',...  34.7 us
    dot_general x1, matrix products, column_term(): lax.dot_general(weight, rows, (((0,), (1,)), ((), ())), preferred_element...  21.7 us
    sub x1, other arithmetic, per_device(): weights = jnp.where(valid[None], jnp.exp(scores - peak[..., None]), 0.0)  18.7 us
    all_gather x1, blocking collectives, per_device(): kv_all = lax.all_gather(kv_piece, 'tp', axis=1, tiled=True)  14.3 us
    ppermute x6, waiting for transfers between devices, gather_ctx(): parts.append(lax.ppermute(value, 'ctx', pairs))  9.82 us
    ppermute x6, starting transfers between devices, gather_ctx(): parts.append(lax.ppermute(value, 'ctx', pairs))  8.9 us
    dot_general x1, matrix products, per_device(): jnp.einsum('chd,kd->hck', query, keys, preferred_element_type=jnp.float32)  8.67 us
  transfers between devices with their start and end apart: 9, of which 3 were waited for; matrix products, arithmetic and copies ran while one was open for 7% of the time, Pallas kernels for 0%

commit v1 on v0

--- a/solution.py
+++ b/solution.py
@@ -10,6 +10,22 @@
 THETA = 5000000.0
 EPS = 1e-05
 NEG = -1e30
+
+
+def find_ranges(packet, group_axis):
+    full_n = lax.axis_size(group_axis)
+    leaves = [(kk, (kk + 1) % full_n) for kk in range(full_n)]
+    cards = [(kk, (kk - 1) % full_n) for kk in range(full_n)]
+    side_arr, prior = ([packet], [packet])
+    for _ in range(full_n // 2):
+        left_arr = lax.ppermute(side_arr[-1], group_axis, perm=leaves)
+        side_arr.append(left_arr)
+    for _ in range((full_n - 1) // 2):
+        y = lax.ppermute(prior[-1], axis_name=group_axis, perm=cards)
+        prior.append(y)
+    s_next = jnp.concatenate([*side_arr[::-1], *prior[1:]], axis=1)
+    arr_next = lax.axis_index(group_axis)
+    return jnp.roll(s_next, (arr_next - full_n // 2) * packet.shape[1], axis=1)
 
 
 def rms_norm(values, gain):
@@ -94,7 +110,7 @@
     ).astype(jnp.bfloat16)
     kv_piece = jnp.dot(x_norm, w_kv, preferred_element_type=jnp.float32).astype(jnp.bfloat16)
     kv_width = kv_piece.shape[1]
-    kv_all = lax.all_gather(kv_piece, "tp", axis=1, tiled=True)
+    kv_all = find_ranges(kv_piece, "tp")
     all_keys = rotate(
         kv_all[:, : KVH * HD].astype(jnp.float32).reshape(span_size, KVH, HD), positions
     ).astype(jnp.bfloat16)

time: 249 us -> 259 us (1.040)
  blocking collectives: 14.3 us -> 0 us
  starting transfers between devices: 9.02 us -> 19.8 us
  local copies, waits for them, and re-layouts: 9.32 us -> 18.9 us
  waiting for transfers between devices: 109 us -> 115 us
    all_gather x1 -> x0, blocking collectives: 14.3 us -> none  [per_device(): kv_all = lax.all_gather(kv_piece, 'tp', axis=1, tiled=True)]
    ppermute x0 -> x7, starting transfers between devices: none -> 10.7 us  [the longest x3 10.7 us: find_ranges(): y = lax.ppermute(prior[-1], axis_name=group_axis, perm=cards)]
    unnamed x20 -> x44, local copies, waits for them, and re-layouts: 0.05 us -> 10.1 us
    ppermute x0 -> x7, waiting for transfers between devices: none -> 4.97 us  [the longest x4 4.97 us: find_ranges(): left_arr = lax.ppermute(side_arr[-1], group_axis, perm=leaves)]
  transfers between devices with their start and end apart: 9 -> 16, of which waited for: 3 -> 6; matrix products, arithmetic and copies ran while one was open for 7% -> 10% of each run, Pallas kernels for 0% -> 0%
where the time goes in v1:
time: 259 us
  waiting for transfers between devices  115 us (44%)
  matrix products  51.5 us (20%)
  other arithmetic  39.3 us (15%)
  starting transfers between devices  19.8 us (8%)
  local copies, waits for them, and re-layouts  18.9 us (7%)
  between operations  14.2 us (5%)
    psum x1, waiting for transfers between devices, per_device(): lax.psum(jnp.dot(attn_rows, w_out, preferred_element_type=jnp.float32).as...  64.4 us
    reduce_scatter x1, waiting for transfers between devices, per_device(): lax.psum_scatter(column_term(hidden, w_down).astype(jnp.bfloat16), 'tp',...  34.5 us
    dot_general x1, matrix products, column_term(): lax.dot_general(weight, rows, (((0,), (1,)), ((), ())), preferred_element...  21.7 us
    sub x1, other arithmetic, per_device(): weights = jnp.where(valid[None], jnp.exp(scores - peak[..., None]), 0.0)  18.7 us
    ppermute x3, starting transfers between devices, find_ranges(): y = lax.ppermute(prior[-1], axis_name=group_axis, perm=cards)  10.7 us
    ppermute x6, waiting for transfers between devices, gather_ctx(): parts.append(lax.ppermute(value, 'ctx', pairs))  10.4 us
    unnamed x44, local copies, waits for them, and re-layouts  10.1 us
    dot_general x1, matrix products, per_device(): jnp.einsum('chd,kd->hck', query, keys, preferred_element_type=jnp.float32)  9.74 us
  transfers between devices with their start and end apart: 16, of which 6 were waited for; matrix products, arithmetic and copies ran while one was open for 10% of the time, Pallas kernels for 0%

profile of v1, /device:TPU:0, one launch (start us, length us, event | category | flops | bytes accessed | tf_op | source)
XLA Modules:
  0.0 258.6 jit_solution(15608545377129027867)
XLA Ops:
  8.6 3.9 %collective-permute-start.2 = (s32[2,8]{1,0:T(2,128)S(1)}, s32[2,8]{1,0:T(2,128)S(1)}, u32[]{:S(2)}, u32[]{:S(2)}) collective-permute-start(s32[2,8]{1,0:T(2,128)S(1)} %pad_add_fusion.1), channel_id=1, source_target_pairs={{0,24},{8,0},{16,8},{24,16},{1,25},{9,1},{17,9},{25,17},{2,26},{10... | collective-permute-start | bytes 200 | tf_op jit(solution)/shard_map/ppermute | solution.py:61
  14.8 2.4 collective-permute-start.5
  25.5 5.1 %pad_add_fusion = pred[256,4352]{0,1:T(8,128)(4,1)} fusion(pred[256,256]{0,1:T(8,128)(4,1)S(1)} %fusion.45, pred[4352]{0:T(1024)(128)(4,1)S(1)} %pad.8.clone), kind=kLoop, calls=%fused_computation.20 | loop fusion | flops 1114112 | bytes 1184000 | tf_op jit(solution)/shard_map/concatenate | solution.py:128
  30.6 10.4 %collective-permute-done.4 = bf16[8,128,256]{2,1,0:T(8,128)(2,1)S(1)} collective-permute-done((bf16[8,128,256]{2,1,0:T(8,128)(2,1)S(1)}, bf16[8,128,256]{2,1,0:T(8,128)(2,1)S(1)}, u32[]{:S(2)}, u32[]{:S(2)}) %collective-permute-start.4) | collective-permute-done | bytes 524320 | tf_op jit(solution)/shard_map/ppermute | solution.py:61
  42.4 2.2 fusion.14
  45.2 2.5 convolution_convert_fusion.2
  50.7 3.5 %collective-permute-start.10 = (bf16[256,128]{0,1:T(8,128)(2,1)S(1)}, bf16[256,128]{0,1:T(8,128)(2,1)}, u32[]{:S(2)}, u32[]{:S(2)}) collective-permute-start(bf16[256,128]{0,1:T(8,128)(2,1)S(1)} %convolution_convert_fusion.2), channel_id=1, source_target_pairs={{0,7},{1,0},{2,1},{3,2},{4,3},{5,4},{6,5},{7,6},{8,15},{9,8},{10,9... | collective-permute-start | bytes 196616 | tf_op jit(solution)/shard_map/ppermute | solution.py:24
  54.2 3.5 %fusion.37 = f32[256,512]{1,0:T(8,128)S(1)} fusion(bf16[4096,512]{1,0:T(8,128)(2,1)} %param.17, bf16[256,4096]{1,0:T(8,128)(2,1)S(1)} %copy-done.2, f32[4096]{0:T(1024)S(1)} %convert_element_type.74, f32[256]{0:T(256)} %copy-done.12), kind=kOutput, calls=%fused_computation.43 | convolution fusion | flops 1077936128 | bytes 6833152 | tf_op jit(solution)/shard_map/dot_general | solution.py:106
  57.9 1.9 collective-permute-done.7
  60.2 3.6 %collective-permute-start.11 = (bf16[256,128]{0,1:T(8,128)(2,1)}, bf16[256,128]{0,1:T(8,128)(2,1)S(1)}, u32[]{:S(2)}, u32[]{:S(2)}) collective-permute-start(bf16[256,128]{0,1:T(8,128)(2,1)} %collective-permute-done.10), channel_id=1, source_target_pairs={{0,7},{1,0},{2,1},{3,2},{4,3},{5,4},{6,5},{7,6},{8,15},{9,8},{10,9... | collective-permute-start | bytes 196616 | tf_op jit(solution)/shard_map/ppermute | solution.py:24
  63.8 2.1 collective-permute-done.8
  66.8 3.5 %collective-permute-start.12 = (bf16[256,128]{0,1:T(8,128)(2,1)S(1)}, bf16[256,128]{0,1:T(8,128)(2,1)S(1)}, u32[]{:S(2)}, u32[]{:S(2)}) collective-permute-start(bf16[256,128]{0,1:T(8,128)(2,1)S(1)} %collective-permute-done.11), channel_id=1, source_target_pairs={{0,7},{1,0},{2,1},{3,2},{4,3},{5,4},{6,5},{7,6},{8,15},{9,8},{10,9... | collective-permute-start | bytes 196616 | tf_op jit(solution)/shard_map/ppermute | solution.py:24
  76.6 2.0 copy.27
  78.6 2.0 copy.26
  82.1 9.7 %fusion.30 = f32[4352,256,4]{1,0,2:T(8,128)} fusion(bf16[256,128]{1,0:T(8,128)(2,1)S(1)} %dynamic-slice_bitcast_fusion, bf16[4096,128]{1,0:T(8,128)(2,1)S(1)} %bitcast.61, bf16[256,4,64]{2,0,1:T(8,128)(2,1)} %get-tuple-element.11, bf16[256,4,64]{2,0,1:T(8,128)(2,1)} %get-tuple-element.10), kind=kOutput, calls=%fused_computation.39 | convolution fusion | flops 1143603200 | bytes 19202048 | tf_op jit(solution)/shard_map/chd,kd->hck/dot_general | solution.py:131
  91.8 18.7 %fusion.59 = (f32[4,256]{1,0:T(4,128)S(1)}, bf16[4,256,4352]{1,2,0:T(8,128)(2,1)}) fusion(f32[4352,256,4]{1,0,2:T(8,128)} %fusion.30, pred[256,4352]{0,1:T(8,128)(4,1)} %pad_add_fusion), kind=kOutput, calls=%fused_computation.106 | output fusion | flops 31199488 | bytes 27856896 | tf_op jit(solution)/shard_map/sub | solution.py:135
  110.5 5.0 %fusion.25 = bf16[256,4,128]{0,2,1:T(8,128)(2,1)S(1)} fusion(bf16[4,256,4352]{1,2,0:T(8,128)(2,1)} %get-tuple-element.23, bf16[256,128]{0,1:T(8,128)(2,1)S(1)} %constant_dynamic-slice_fusion.1, bf16[4096,128]{0,1:T(8,128)(2,1)S(1)} %copy-done.8, f32[256,4]{0,1:T(4,128)S(1)} %bitcast.70), kind=kOutput, calls=%fused_computation.33 | convolution fusion | flops 1143341056 | bytes 10293248 | tf_op jit(solution)/shard_map/hck,kd->hcd/dot_general | solution.py:137
  115.6 2.6 %convolution_convert_fusion = bf16[256,4096]{1,0:T(8,128)(2,1)} fusion(bf16[256,512]{0,1:T(8,128)(2,1)S(1)} %bitcast.65, bf16[512,4096]{1,0:T(8,128)(2,1)S(1)} %copy-done.4), kind=kOutput, calls=%fused_computation.17 | convolution fusion | flops 1074790400 | bytes 6553600 | tf_op jit(solution)/shard_map/dot_general | solution.py:147
  118.3 64.4 %all-reduce.2.cloned.1.call-done = bf16[256,4096]{1,0:T(8,128)(2,1)} async-done(((bf16[256,4096]{1,0:T(8,128)(2,1)}), bf16[256,4096]{1,0:T(8,128)(2,1)}) %all-reduce.2.cloned.1.call-update) | async-done | bytes 2097168 | tf_op jit(solution)/shard_map/psum | solution.py:146
  182.6 2.5 fusion.11
  186.5 6.4 %fusion.35 = f32[256,1376]{0,1:T(8,128)S(1)} fusion(bf16[4096,1376]{0,1:T(8,128)(2,1)} %param.20, bf16[256,4096]{1,0:T(8,128)(2,1)S(1)} %get-tuple-element.5, f32[4096]{0:T(1024)S(1)} %convert_element_type.87, f32[256]{0:T(256)S(1)} %add_rsqrt_fusion), kind=kOutput, calls=%fused_computation.42 | convolution fusion | flops 2889875456 | bytes 14795776 | tf_op jit(solution)/shard_map/dot_general | solution.py:152
  192.9 21.7 %fusion.10 = bf16[4096,256]{0,1:T(8,128)(2,1)} fusion(bf16[1376,4096]{1,0:T(8,128)(2,1)} %param.22, bf16[4096,1376]{0,1:T(8,128)(2,1)} %param.21, f32[256,1376]{0,1:T(8,128)S(1)} %fusion.35, bf16[256,4096]{1,0:T(8,128)(2,1)} %copy-done.6, f32[4096]{0:T(1024)S(1)} %convert_element_type.87, f32[256]{0:T(256)S(1)} %add_rsqrt_fusion), kind=kOutput, calls=%fused_computation.19 | convolution fusion | flops 5778718720 | bytes 28165120 | tf_op jit(solution)/shard_map/dot_general | solution.py:52
  215.7 34.5 %reduce-scatter.2.cloned.1.call-done = bf16[512,256]{0,1:T(8,128)(2,1)} async-done(((bf16[4096,256]{0,1:T(8,128)(2,1)}), bf16[512,256]{0,1:T(8,128)(2,1)}) %reduce-scatter.2.cloned.1.call-update) | async-done | bytes 262160 | tf_op jit(solution)/shard_map/reduce_scatter | solution.py:155
  250.3 1.8 fusion.41
  (101 shorter events, 28.4 us)
Async XLA Ops:
  7.2 38.0 %copy-start = (bf16[4096,128]{1,0:T(8,128)(2,1)S(1)}, bf16[4096,128]{1,0:T(8,128)(2,1)}, u32[]{:S(2)}) copy-start(bf16[4096,128]{1,0:T(8,128)(2,1)} %param.18) | copy-start | bytes 3145732
  7.2 35.2 %all-gather.2.cloned.1.call-start = ((), (), s32[]{:S(2)}) async-start(), calls=%async_computation.1 | async-start | bytes 2359296 | tf_op jit(solution)/shard_map/all_gather | solution.py:103
  7.9 174.7 %all-reduce.2.cloned.1.call-start = ((), (), s32[]{:S(2)}) async-start(), calls=%async_computation.2 | async-start | bytes 4194304 | tf_op jit(solution)/shard_map/psum | solution.py:146
  8.6 15.2 %collective-permute-start.2 = (s32[2,8]{1,0:T(2,128)S(1)}, s32[2,8]{1,0:T(2,128)S(1)}, u32[]{:S(2)}, u32[]{:S(2)}) collective-permute-start(s32[2,8]{1,0:T(2,128)S(1)} %pad_add_fusion.1), channel_id=1, source_target_pairs={{0,24},{8,0},{16,8},{24,16},{1,25},{9,1},{17,9},{25,17},{2,26},{10... | collective-permute-start | bytes 200 | tf_op jit(solution)/shard_map/ppermute | solution.py:61
  12.5 11.4 %collective-permute-start.1 = (s32[2,8]{1,0:T(2,128)S(1)}, s32[2,8]{1,0:T(2,128)S(1)}, u32[]{:S(2)}, u32[]{:S(2)}) collective-permute-start(s32[2,8]{1,0:T(2,128)S(1)} %pad_add_fusion.1), channel_id=1, source_target_pairs={{0,16},{8,24},{16,0},{24,8},{1,17},{9,25},{17,1},{25,9},{2,18},{10... | collective-permute-start | bytes 200 | tf_op jit(solution)/shard_map/ppermute | solution.py:61
  13.0 10.9 %collective-permute-start = (s32[2,8]{1,0:T(2,128)S(1)}, s32[2,8]{1,0:T(2,128)S(1)}, u32[]{:S(2)}, u32[]{:S(2)}) collective-permute-start(s32[2,8]{1,0:T(2,128)S(1)} %pad_add_fusion.1), channel_id=1, source_target_pairs={{0,8},{8,16},{16,24},{24,0},{1,9},{9,17},{17,25},{25,1},{2,10},{10... | collective-permute-start | bytes 200 | tf_op jit(solution)/shard_map/ppermute | solution.py:61
  14.8 15.8 %collective-permute-start.5 = (bf16[8,128,256]{2,1,0:T(8,128)(2,1)S(1)}, bf16[8,128,256]{2,1,0:T(8,128)(2,1)S(1)}, u32[]{:S(2)}, u32[]{:S(2)}) collective-permute-start(bf16[8,128,256]{2,1,0:T(8,128)(2,1)S(1)} %pad_maximum_fusion.1), channel_id=1, source_target_pairs={{0,24},{8,0},{16,8},{24,16},{1,25},{9,1},{17,9},{25,17},{2,26},{10... | collective-permute-start | bytes 1572872 | tf_op jit(solution)/shard_map/ppermute | solution.py:61
  17.2 23.8 %collective-permute-start.4 = (bf16[8,128,256]{2,1,0:T(8,128)(2,1)S(1)}, bf16[8,128,256]{2,1,0:T(8,128)(2,1)S(1)}, u32[]{:S(2)}, u32[]{:S(2)}) collective-permute-start(bf16[8,128,256]{2,1,0:T(8,128)(2,1)S(1)} %pad_maximum_fusion.1), channel_id=1, source_target_pairs={{0,16},{8,24},{16,0},{24,8},{1,17},{9,25},{17,1},{25,9},{2,18},{10... | collective-permute-start | bytes 1572872 | tf_op jit(solution)/shard_map/ppermute | solution.py:61
  23.9 17.1 %collective-permute-start.3 = (bf16[8,128,256]{2,1,0:T(8,128)(2,1)S(1)}, bf16[8,128,256]{2,1,0:T(8,128)(2,1)S(1)}, u32[]{:S(2)}, u32[]{:S(2)}) collective-permute-start(bf16[8,128,256]{2,1,0:T(8,128)(2,1)S(1)} %pad_maximum_fusion.1), channel_id=1, source_target_pairs={{0,8},{8,16},{16,24},{24,0},{1,9},{9,17},{17,25},{25,1},{2,10},{10... | collective-permute-start | bytes 1572872 | tf_op jit(solution)/shard_map/ppermute | solution.py:61
  42.4 5.5 %copy-start.3 = (bf16[32,128,256]{2,1,0:T(8,128)(2,1)S(1)}, bf16[32,128,256]{2,1,0:T(8,128)(2,1)}, u32[]{:S(2)}) copy-start(bf16[32,128,256]{2,1,0:T(8,128)(2,1)} %pad_maximum_fusion) | copy-start | bytes 6291460
  47.7 6.5 %copy-start.2 = (bf16[256,4096]{1,0:T(8,128)(2,1)S(1)}, bf16[256,4096]{1,0:T(8,128)(2,1)}, u32[]{:S(2)}) copy-start(bf16[256,4096]{1,0:T(8,128)(2,1)} %all-gather.2.cloned.1.call-done) | copy-start | bytes 6291460
  47.8 6.5 %collective-permute-start.6 = (bf16[256,128]{0,1:T(8,128)(2,1)S(1)}, bf16[256,128]{0,1:T(8,128)(2,1)S(1)}, u32[]{:S(2)}, u32[]{:S(2)}) collective-permute-start(bf16[256,128]{0,1:T(8,128)(2,1)S(1)} %convolution_convert_fusion.2), channel_id=1, source_target_pairs={{0,1},{1,2},{2,3},{3,4},{4,5},{5,6},{6,7},{7,0},{8,9},{9,10},{10,1... | collective-permute-start | bytes 196616 | tf_op jit(solution)/shard_map/ppermute | solution.py:21
  50.7 9.5 %collective-permute-start.10 = (bf16[256,128]{0,1:T(8,128)(2,1)S(1)}, bf16[256,128]{0,1:T(8,128)(2,1)}, u32[]{:S(2)}, u32[]{:S(2)}) collective-permute-start(bf16[256,128]{0,1:T(8,128)(2,1)S(1)} %convolution_convert_fusion.2), channel_id=1, source_target_pairs={{0,7},{1,0},{2,1},{3,2},{4,3},{5,4},{6,5},{7,6},{8,15},{9,8},{10,9... | collective-permute-start | bytes 196616 | tf_op jit(solution)/shard_map/ppermute | solution.py:24
  54.2 5.6 %collective-permute-start.7 = (bf16[256,128]{0,1:T(8,128)(2,1)S(1)}, bf16[256,128]{0,1:T(8,128)(2,1)}, u32[]{:S(2)}, u32[]{:S(2)}) collective-permute-start(bf16[256,128]{0,1:T(8,128)(2,1)S(1)} %collective-permute-done.6), channel_id=1, source_target_pairs={{0,1},{1,2},{2,3},{3,4},{4,5},{5,6},{6,7},{7,0},{8,9},{9,10},{10,1... | collective-permute-start | bytes 196616 | tf_op jit(solution)/shard_map/ppermute | solution.py:21
  59.8 6.0 %collective-permute-start.8 = (bf16[256,128]{0,1:T(8,128)(2,1)}, bf16[256,128]{0,1:T(8,128)(2,1)S(1)}, u32[]{:S(2)}, u32[]{:S(2)}) collective-permute-start(bf16[256,128]{0,1:T(8,128)(2,1)} %collective-permute-done.7), channel_id=1, source_target_pairs={{0,1},{1,2},{2,3},{3,4},{4,5},{5,6},{6,7},{7,0},{8,9},{9,10},{10,1... | collective-permute-start | bytes 196616 | tf_op jit(solution)/shard_map/ppermute | solution.py:21
  60.2 6.6 %collective-permute-start.11 = (bf16[256,128]{0,1:T(8,128)(2,1)}, bf16[256,128]{0,1:T(8,128)(2,1)S(1)}, u32[]{:S(2)}, u32[]{:S(2)}) collective-permute-start(bf16[256,128]{0,1:T(8,128)(2,1)} %collective-permute-done.10), channel_id=1, source_target_pairs={{0,7},{1,0},{2,1},{3,2},{4,3},{5,4},{6,5},{7,6},{8,15},{9,8},{10,9... | collective-permute-start | bytes 196616 | tf_op jit(solution)/shard_map/ppermute | solution.py:24
  65.8 5.5 %collective-permute-start.9 = (bf16[256,128]{0,1:T(8,128)(2,1)S(1)}, bf16[256,128]{0,1:T(8,128)(2,1)S(1)}, u32[]{:S(2)}, u32[]{:S(2)}) collective-permute-start(bf16[256,128]{0,1:T(8,128)(2,1)S(1)} %collective-permute-done.8), channel_id=1, source_target_pairs={{0,1},{1,2},{2,3},{3,4},{4,5},{5,6},{6,7},{7,0},{8,9},{9,10},{10,1... | collective-permute-start | bytes 196616 | tf_op jit(solution)/shard_map/ppermute | solution.py:21
  66.8 6.4 %collective-permute-start.12 = (bf16[256,128]{0,1:T(8,128)(2,1)S(1)}, bf16[256,128]{0,1:T(8,128)(2,1)S(1)}, u32[]{:S(2)}, u32[]{:S(2)}) collective-permute-start(bf16[256,128]{0,1:T(8,128)(2,1)S(1)} %collective-permute-done.11), channel_id=1, source_target_pairs={{0,7},{1,0},{2,1},{3,2},{4,3},{5,4},{6,5},{7,6},{8,15},{9,8},{10,9... | collective-permute-start | bytes 196616 | tf_op jit(solution)/shard_map/ppermute | solution.py:24
  71.3 10.7 %copy-start.5 = (bf16[32,128,128]{2,1,0:T(8,128)(2,1)S(1)}, bf16[32,128,128]{2,1,0:T(8,128)(2,1)}, u32[]{:S(2)}) copy-start(bf16[32,128,128]{2,1,0:T(8,128)(2,1)} %get-tuple-element.7) | copy-start | bytes 3145732
  91.8 18.7 %copy-start.8 = (bf16[4096,128]{0,1:T(8,128)(2,1)S(1)}, bf16[4096,128]{0,1:T(8,128)(2,1)}, u32[]{:S(2)}) copy-start(bf16[4096,128]{0,1:T(8,128)(2,1)} %copy.25) | copy-start | bytes 3145732
  118.2 132.1 %reduce-scatter.2.cloned.1.call-start = ((), (), s32[]{:S(2)}) async-start(), calls=%async_computation.3 | async-start | bytes 2359296 | tf_op jit(solution)/shard_map/reduce_scatter | solution.py:155
  192.9 22.0 %copy-start.7 = (bf16[256,512]{0,1:T(8,128)(2,1)S(1)}, bf16[256,512]{0,1:T(8,128)(2,1)}, u32[]{:S(2)}) copy-start(bf16[256,512]{0,1:T(8,128)(2,1)} %get-tuple-element.14) | copy-start | bytes 786436
  192.9 22.0 %copy-start.11 = (pred[256]{0:T(512)(128)(4,1)S(1)}, pred[256]{0:T(512)(128)(4,1)}, u32[]{:S(2)}) copy-start(pred[256]{0:T(512)(128)(4,1)} %copy-done.10) | copy-start | bytes 772
  192.9 59.2 %copy-start.1 = (bf16[4096,128]{1,0:T(8,128)(2,1)S(1)}, bf16[4096,128]{1,0:T(8,128)(2,1)}, u32[]{:S(2)}) copy-start(bf16[4096,128]{1,0:T(8,128)(2,1)} %param.18) | copy-start | bytes 3145732
  (5 other events, 11.8 us)
Sparse Core Ops, SparseCore 0:
  9.6 31.7 all-gather.1
  118.3 64.2 all-reduce.1
  214.8 35.3 reduce-scatter.1
